TPU v7x, 256 devices: a whole 4x4x8 slice. The times are simulated.
256 devices in a mesh: seq: 32 (over x, z), tp: 8 (over y, core).
Axes of the slice: x: 4, y: 4, z: 8, core: 2. Of those that a mesh axis runs over, the one named last changes fastest.
Arguments:
- tokens: bfloat16 [32768, 2048], P('seq', 'tp'), may hold values from -6 to 6
- w_inner: bfloat16 [2048, 2, 4096], P('seq', None, 'tp'), may hold values from -0.125 to 0.125
- w_states: bfloat16 [2048, 256], P('seq'), may hold values from -0.125 to 0.125
- w_step: bfloat16 [2048, 64], P('seq', 'tp'), may hold values from -0.125 to 0.125
- conv_inner: float32 [4, 4096], P(None, 'tp'), may hold values from -3 to 3
- conv_states: float32 [4, 256], replicated, may hold values from -3 to 3
- decay_rate: float32 [64], P('tp'), may hold values from 0 to 1, as said below
- step_bias: float32 [64], P('tp'), may hold values from -1 to 0.5
- skip_gain: float32 [64], P('tp'), may hold values from 0.5 to 1.5
- norm_gain: float32 [4096], P('tp'), may hold values from 0.5 to 1.5
- w_output: bfloat16 [4096, 2048], P('tp', 'seq'), may hold values from -0.09375 to 0.09375
- block_owner: int32 [128], replicated, may hold values from 0 to 19, as said below
- lengths: int32 [20], replicated, may hold values from 1 to 16384, as said below
Outputs:
- mixed: bfloat16 [32768, 2048], P('seq', 'tp')
Inputs may be any that keep to these rules, and one draw needn't show every extreme that they name: `block_owner`: each prompt's blocks are consecutive, prompt r has ceil(lengths[r] / 256) of them, and the prompts follow one another in an order drawn afresh; one prompt has 64 blocks and is neither the first nor the last in that order. `lengths`: one prompt has exactly 16384 tokens. `decay_rate`: Positive.
All inputs are finite; a program needn't handle non-finite values.
Results may differ from a plain program's by a relative error of at most 0.0075.
Values may be sent and summed in bfloat16 or wider, within the bound.
No kernel may reach another device: no remote copies, remote signals or barrier semaphores. Data moves between devices by JAX's collectives and lax.ppermute only.
A program may use at most 64 MiB of HBM per device.

v0:
```python
import jax
import jax.numpy as jnp
from jax import lax
from jax.sharding import PartitionSpec as P

BLOCK = 256
LONGEST = 64


def passed_along(value, axis, by):
    count = lax.axis_size(axis)
    pairs = [(i, i + by) for i in range(count) if 0 <= i + by < count]
    return lax.ppermute(value, axis, pairs)


def convolve(values, edge_rows, weights, in_block, carry_on):
    lag_rows = weights.shape[0] - 1
    row_total = values.shape[0]
    widened = jnp.concatenate([edge_rows, values], axis=0).astype(jnp.float32)
    total = jnp.zeros(values.shape, jnp.float32)
    for offset in range(weights.shape[0]):
        shifted = widened[lag_rows - offset : lag_rows - offset + row_total]
        keeping = (in_block >= offset) | carry_on
        total = total + jnp.where(keeping[:, None], shifted, 0.0) * weights[offset]
    return jax.nn.silu(total).astype(jnp.bfloat16)


def on_device(
    tokens,
    w_inner,
    w_states,
    w_step,
    conv_inner,
    conv_states,
    decay_rate,
    step_bias,
    skip_gain,
    norm_gain,
    w_output,
    block_owner,
    lengths,
):
    row_count = tokens.shape[0]
    local_blocks = row_count // BLOCK
    total_blocks = block_owner.shape[0]
    heads_here = w_step.shape[1]
    inner_here = w_inner.shape[2]
    state_size = w_states.shape[1] // 2
    head_size = inner_here // heads_here
    lag_rows = conv_inner.shape[0] - 1
    block_ids = jnp.arange(total_blocks, dtype=jnp.int32)
    same_owner = block_owner[:, None] == block_owner[None, :]
    first_block = jnp.min(jnp.where(same_owner, block_ids[None, :], total_blocks), axis=1)
    starting = (first_block == block_ids).astype(jnp.int32)
    request_ids = jnp.arange(lengths.shape[0], dtype=jnp.int32)
    own_length = jnp.sum(
        jnp.where(block_owner[:, None] == request_ids[None, :], lengths[None, :], 0), axis=1
    )
    valid_rows = jnp.clip(own_length - (block_ids - first_block) * BLOCK, 0, BLOCK)
    seq_index = lax.axis_index("seq")
    local_start = lax.dynamic_slice_in_dim(starting, seq_index * local_blocks, local_blocks)
    local_valid = lax.dynamic_slice_in_dim(valid_rows, seq_index * local_blocks, local_blocks)
    in_block = jnp.arange(row_count, dtype=jnp.int32) % BLOCK
    carry_on = jnp.repeat(local_start == 0, BLOCK)
    whole = lax.all_gather(tokens, "tp", axis=1, tiled=True)
    first_cols = jnp.concatenate([w_inner[:, 1, :], w_states, w_step], axis=1)
    first_weights = lax.all_gather(first_cols, "seq", axis=0, tiled=True)
    gate_weights = lax.all_gather(w_inner[:, 0, :], "seq", axis=0, tiled=True)
    first_sum = jnp.dot(whole, first_weights, preferred_element_type=jnp.float32)
    projected = first_sum.astype(jnp.bfloat16)
    x_in = projected[:, :inner_here]
    bc_in = projected[:, inner_here : inner_here + 2 * state_size]
    step_raw = projected[:, inner_here + 2 * state_size :]
    gate_in = jnp.dot(whole, gate_weights, preferred_element_type=jnp.float32).astype(jnp.bfloat16)
    edge_inner, edge_states = passed_along(
        (x_in[row_count - lag_rows :], bc_in[row_count - lag_rows :]), "seq", 1
    )
    x_conv = convolve(x_in, edge_inner, conv_inner, in_block, carry_on)
    bc_conv = convolve(bc_in, edge_states, conv_states, in_block, carry_on)
    step_size = jax.nn.softplus(step_raw.astype(jnp.float32) + step_bias)
    log_decay = -decay_rate * step_size
    x_heads = x_conv.reshape(local_blocks, BLOCK, heads_here, head_size)
    b_rows = bc_conv[:, :state_size].reshape(local_blocks, BLOCK, state_size)
    c_rows = bc_conv[:, state_size:].reshape(local_blocks, BLOCK, state_size)
    step_blocks = step_size.reshape(local_blocks, BLOCK, heads_here)
    cumulative = jnp.cumsum(log_decay.reshape(local_blocks, BLOCK, heads_here), axis=1)
    causal = jnp.arange(BLOCK)[:, None] >= jnp.arange(BLOCK)[None, :]
    spread = cumulative[:, :, None, :] - cumulative[:, None, :, :]
    decays = jnp.exp(jnp.where(causal[None, :, :, None], spread, -jnp.inf))
    intersection = jnp.einsum("cin,cjn->cij", c_rows, b_rows, preferred_element_type=jnp.float32)
    mixing = (decays * intersection[:, :, :, None] * step_blocks[:, None, :, :]).astype(
        jnp.bfloat16
    )
    y_inner = jnp.einsum("cijh,cjhp->cihp", mixing, x_heads, preferred_element_type=jnp.float32)
    final_log = cumulative[:, -1, :]
    tail_weight = jnp.exp(final_log[:, None, :] - cumulative) * step_blocks
    weighted_b = (tail_weight[:, :, :, None] * b_rows.astype(jnp.float32)[:, :, None, :]).astype(
        jnp.bfloat16
    )
    fresh = jnp.einsum("cjhn,cjhp->chnp", weighted_b, x_heads, preferred_element_type=jnp.float32)
    keep_flag = jnp.where(local_start == 1, 0.0, 1.0).astype(jnp.float32)
    block_gain_each = jnp.exp(final_log) * keep_flag[:, None]
    block_gain = jnp.ones((heads_here,), jnp.float32)
    block_state = jnp.zeros((heads_here, state_size, head_size), jnp.float32)
    gains_in, states_in = ([], [])
    for block in range(local_blocks):
        gains_in.append(block_gain * keep_flag[block])
        states_in.append(block_state * keep_flag[block])
        block_gain = block_gain * block_gain_each[block]
        block_state = block_gain_each[block][:, None, None] * block_state + fresh[block]

    def packed(gain, state):
        rows = jnp.broadcast_to(gain[:, None, None], (heads_here, 1, head_size))
        return jnp.concatenate([state, rows], axis=1)

    prefix = passed_along(packed(block_gain, block_state), "seq", 1)
    needed = min(-(-(LONGEST - 1) // local_blocks), lax.axis_size("seq") - 1)
    reach = 1
    while reach < needed:
        earlier = passed_along(prefix, "seq", reach)
        gain_now = prefix[:, state_size:, :1]
        prefix = jnp.concatenate(
            [
                gain_now * earlier[:, :state_size] + prefix[:, :state_size],
                gain_now * earlier[:, state_size:],
            ],
            axis=1,
        )
        reach *= 2
    entering = prefix[:, :state_size]
    incoming_all = jnp.stack(gains_in)[:, :, None, None] * entering[None] + jnp.stack(states_in)
    incoming_half = incoming_all.astype(jnp.bfloat16)
    y_carry = jnp.exp(cumulative)[:, :, :, None] * jnp.einsum(
        "cin,chnp->cihp", c_rows, incoming_half, preferred_element_type=jnp.float32
    )
    y_total = (y_inner + y_carry).reshape(row_count, inner_here) + jnp.repeat(skip_gain, head_size)[
        None, :
    ] * x_conv.astype(jnp.float32)
    gated = y_total * jax.nn.silu(gate_in.astype(jnp.float32))
    squares = jnp.sum(gated * gated, axis=1)
    scaled = (gated * norm_gain).astype(jnp.bfloat16)
    partial_out = jnp.dot(
        scaled,
        lax.all_gather(w_output, "seq", axis=1, tiled=True),
        preferred_element_type=jnp.float32,
    )
    tp_count = lax.axis_size("tp")
    cols_here = partial_out.shape[1] // tp_count
    square_rows = jnp.tile(squares.reshape(row_count // cols_here, cols_here), (1, tp_count))
    summed = lax.psum_scatter(
        jnp.concatenate([partial_out, square_rows], axis=0), "tp", scatter_dimension=1, tiled=True
    )
    square_mean = summed[row_count:].reshape(row_count) / (inner_here * tp_count)
    mixed = summed[:row_count] * lax.rsqrt(square_mean + 1e-05)[:, None]
    live = in_block < jnp.repeat(local_valid, BLOCK)
    return jnp.where(live[:, None], mixed, 0.0).astype(jnp.bfloat16)


def solution(mesh):
    return jax.shard_map(
        on_device,
        mesh=mesh,
        in_specs=(
            P("seq", "tp"),
            P("seq", None, "tp"),
            P("seq", None),
            P("seq", "tp"),
            P(None, "tp"),
            P(),
            P("tp"),
            P("tp"),
            P("tp"),
            P("tp"),
            P("tp", "seq"),
            P(),
            P(),
        ),
        out_specs=P("seq", "tp"),
        check_vma=False,
    )
```

profile of v0, /device:TPU:1, one launch (start us, length us, event | category | flops | bytes accessed | tf_op | source)
XLA Modules:
  0.0 382.6 jit_solution(7631663439975435024)
XLA Ops:
  6.5 0.8 copy.88
  7.3 1.2 fusion.70
  8.6 1.4 pad_maximum_fusion.5
  10.0 0.7 all-gather.8.cloned.1.call-update
  10.8 0.6 copy.109
  11.5 0.9 select_reduce_fusion
  13.2 0.7 neg.19
  14.5 0.8 fusion.72
  15.3 0.9 fusion.71
  16.2 74.5 %all-gather.6.cloned.1.call-done = bf16[2048,776]{1,0:T(8,128)(2,1)} async-done(((bf16[64,776]{1,0:T(8,128)(2,1)}), bf16[2048,776]{1,0:T(8,128)(2,1)}) %all-gather.6.cloned.1.call-update) | async-done | bytes 3178512 | tf_op jit(solution)/shard_map/all_gather | solution.py:67
  90.6 41.1 %all-gather.8.cloned.1.call-done = bf16[1024,2048]{1,0:T(8,128)(2,1)} async-done(((bf16[1024,256]{1,0:T(8,128)(2,1)}), bf16[1024,2048]{1,0:T(8,128)(2,1)}) %all-gather.8.cloned.1.call-update) | async-done | bytes 4194320 | tf_op jit(solution)/shard_map/all_gather | solution.py:65
  131.7 7.8 %convert_bitcast_fusion = bf16[1024,776]{1,0:T(8,128)(2,1)S(1)} fusion(bf16[2048,776]{1,0:T(8,128)(2,1)} %all-gather.6.cloned.1.call-done, bf16[1024,2048]{1,0:T(8,128)(2,1)} %all-gather.8.cloned.1.call-done), kind=kOutput, calls=%fused_computation.36 | convolution fusion | flops 3255574528 | bytes 8962048 | tf_op jit(solution)/shard_map/dot_general | solution.py:69
  139.6 3.2 collective-permute-start.1
  142.7 3.2 collective-permute-start
  146.6 2.3 reduce-window.6
  150.0 2.3 broadcast_multiply_fusion.3
  152.6 1.4 multiply_convert_fusion.9
  154.0 0.7 fusion.69
  154.8 0.8 convert_element_type.64
  156.0 2.2 multiply_convert_fusion.5
  158.2 1.1 reshape.173
  159.3 2.0 copy.95
  161.3 2.8 fusion.11
  164.4 4.0 %collective-permute-start.2 = (f32[8,129,64]{1,2,0:T(8,128)S(1)}, f32[8,129,64]{1,2,0:T(8,128)}, u32[]{:S(2)}, u32[]{:S(2)}) collective-permute-start(f32[8,129,64]{1,2,0:T(8,128)S(1)} %pad_maximum_fusion.1), channel_id=1, source_target_pairs={{0,8},{8,16},{16,24},{24,32},{32,40},{40,48},{48,56},{56,64},{64,7... | collective-permute-start | bytes 792584 | tf_op jit(solution)/shard_map/ppermute | solution.py:13
  168.4 10.1 %collective-permute-done.2 = f32[8,129,64]{1,2,0:T(8,128)} collective-permute-done((f32[8,129,64]{1,2,0:T(8,128)S(1)}, f32[8,129,64]{1,2,0:T(8,128)}, u32[]{:S(2)}, u32[]{:S(2)}) %collective-permute-start.2) | collective-permute-done | bytes 264224 | tf_op jit(solution)/shard_map/ppermute | solution.py:13
  178.5 4.2 %collective-permute-start.3 = (f32[8,129,64]{1,2,0:T(8,128)}, f32[8,129,64]{1,2,0:T(8,128)S(1)}, u32[]{:S(2)}, u32[]{:S(2)}) collective-permute-start(f32[8,129,64]{1,2,0:T(8,128)} %collective-permute-done.2), channel_id=1, source_target_pairs={{0,8},{8,16},{16,24},{24,32},{32,40},{40,48},{48,56},{56,64},{64,7... | collective-permute-start | bytes 792584 | tf_op jit(solution)/shard_map/ppermute | solution.py:13
  184.2 0.9 slice_reduce_fusion.4
  185.1 13.7 %collective-permute-done.3 = f32[8,129,64]{1,2,0:T(8,128)S(1)} collective-permute-done((f32[8,129,64]{1,2,0:T(8,128)}, f32[8,129,64]{1,2,0:T(8,128)S(1)}, u32[]{:S(2)}, u32[]{:S(2)}) %collective-permute-start.3) | collective-permute-done | bytes 264224 | tf_op jit(solution)/shard_map/ppermute | solution.py:13
  198.8 0.8 copy-done.3
  199.6 1.0 slice_add_fusion
  200.6 1.1 slice_multiply_fusion.7
  201.8 7.5 %collective-permute-start.4 = (f32[8,129,64]{1,2,0:T(8,128)S(1)}, f32[8,129,64]{1,2,0:T(8,128)S(1)}, u32[]{:S(2)}, u32[]{:S(2)}) collective-permute-start(f32[8,129,64]{1,2,0:T(8,128)S(1)} %pad_maximum_fusion.2), channel_id=1, source_target_pairs={{0,16},{8,24},{16,32},{24,40},{32,48},{40,56},{48,64},{56,72},{64,... | collective-permute-start | bytes 792584 | tf_op jit(solution)/shard_map/ppermute | solution.py:13
  209.6 21.6 %collective-permute-done.4 = f32[8,129,64]{1,2,0:T(8,128)S(1)} collective-permute-done((f32[8,129,64]{1,2,0:T(8,128)S(1)}, f32[8,129,64]{1,2,0:T(8,128)S(1)}, u32[]{:S(2)}, u32[]{:S(2)}) %collective-permute-start.4) | collective-permute-done | bytes 264224 | tf_op jit(solution)/shard_map/ppermute | solution.py:13
  231.4 9.2 %collective-permute-start.5 = (f32[8,129,64]{1,2,0:T(8,128)S(1)}, f32[8,129,64]{1,2,0:T(8,128)S(1)}, u32[]{:S(2)}, u32[]{:S(2)}) collective-permute-start(f32[8,129,64]{1,2,0:T(8,128)S(1)} %pad_maximum_fusion.3), channel_id=1, source_target_pairs={{0,32},{8,40},{16,48},{24,56},{32,64},{40,72},{48,80},{56,88},{64,... | collective-permute-start | bytes 792584 | tf_op jit(solution)/shard_map/ppermute | solution.py:13
  241.0 23.4 %collective-permute-done.5 = f32[8,129,64]{1,2,0:T(8,128)S(1)} collective-permute-done((f32[8,129,64]{1,2,0:T(8,128)S(1)}, f32[8,129,64]{1,2,0:T(8,128)S(1)}, u32[]{:S(2)}, u32[]{:S(2)}) %collective-permute-start.5) | collective-permute-done | bytes 264224 | tf_op jit(solution)/shard_map/ppermute | solution.py:13
  264.7 7.4 %collective-permute-start.6 = (f32[8,129,64]{1,2,0:T(8,128)S(1)}, f32[8,129,64]{1,2,0:T(8,128)S(1)}, u32[]{:S(2)}, u32[]{:S(2)}) collective-permute-start(f32[8,129,64]{1,2,0:T(8,128)S(1)} %pad_maximum_fusion.4), channel_id=1, source_target_pairs={{0,64},{8,72},{16,80},{24,88},{32,96},{40,104},{48,112},{56,120},{... | collective-permute-start | bytes 792584 | tf_op jit(solution)/shard_map/ppermute | solution.py:13
  272.1 1.9 broadcast_multiply_fusion.1
  274.2 8.5 %collective-permute-done.6 = f32[8,129,64]{1,2,0:T(8,128)S(1)} collective-permute-done((f32[8,129,64]{1,2,0:T(8,128)S(1)}, f32[8,129,64]{1,2,0:T(8,128)S(1)}, u32[]{:S(2)}, u32[]{:S(2)}) %collective-permute-start.6) | collective-permute-done | bytes 264224 | tf_op jit(solution)/shard_map/ppermute | solution.py:13
  284.0 2.4 bitcast_add_fusion
  286.4 2.8 copy.104
  289.2 4.8 %reshape.172 = f32[1024,512]{1,0:T(8,128)} reshape(f32[4,256,8,64]{3,2,1,0:T(8,128)} %copy.104) | data formatting | bytes 4194304 | tf_op jit(solution)/shard_map/reshape | solution.py:136
  294.0 6.4 %multiply_reduce_fusion = (f32[1024]{0:T(1024)S(1)}, f32[1024,512]{1,0:T(8,128)S(1)}) fusion(bf16[1024,2048]{1,0:T(8,128)(2,1)} %all-gather.8.cloned.1.call-done, bf16[2048,1,512]{2,0,1:T(8,128)(2,1)} %all-gather.12.cloned.1.call-done, f32[1024,512]{1,0:T(8,128)} %reshape.172, bf16[1024,512]{1,0:T(8,128)(2,1)S(1)} %multiply_convert_fusion.5, f32[512]{0:T(512)S(1)} %mul.490), kind=kOutput, calls=%fused_computation.31 | convolution fusion | flops 2153774080 | bytes 11540480 | tf_op jit(solution)/shard_map/dot_general | solution.py:74
  300.5 7.9 %all-gather.10.cloned.1.call-done = bf16[512,2048]{0,1:T(8,128)(2,1)} async-done(((bf16[512,64]{0,1:T(8,128)(2,1)}), bf16[512,2048]{0,1:T(8,128)(2,1)}) %all-gather.10.cloned.1.call-update) | async-done | bytes 2097168 | tf_op jit(solution)/shard_map/all_gather | solution.py:144
  308.4 4.0 %fusion.28 = f32[1024,2048]{1,0:T(8,128)S(1)} fusion(bf16[512,2048]{0,1:T(8,128)(2,1)} %all-gather.10.cloned.1.call-done, f32[1024,512]{1,0:T(8,128)S(1)} %get-tuple-element.41, f32[512]{0:T(512)S(1)} %copy-done.4), kind=kOutput, calls=%fused_computation.40 | convolution fusion | flops 2148532224 | bytes 12584960 | tf_op jit(solution)/shard_map/dot_general | solution.py:142
  312.4 3.9 %pad_maximum_fusion = f32[1028,2048]{1,0:T(8,128)} fusion(f32[4,2048]{1,0:T(4,128)S(1)} %bitcast.119, f32[1024,2048]{1,0:T(8,128)S(1)} %fusion.28), kind=kLoop, calls=%fused_computation | loop fusion | flops 2105344 | bytes 16842752 | tf_op jit(solution)/shard_map/concatenate | solution.py:151
  317.2 55.8 %reduce-scatter.2.cloned.1.call-done = f32[1028,256]{1,0:T(8,128)} async-done(((f32[1028,2048]{1,0:T(8,128)}), f32[1028,256]{1,0:T(8,128)}) %reduce-scatter.2.cloned.1.call-update) | async-done | bytes 1052688 | tf_op jit(solution)/shard_map/reduce_scatter | solution.py:150
  373.0 0.7 fusion.50
  373.7 2.4 fusion.30
  (102 shorter events, 8.6 us)
Async XLA Ops:
  6.5 84.1 %all-gather.6.cloned.1.call-start = ((), (), s32[]{:S(2)}) async-start(), calls=%async_computation.1 | async-start | bytes 3784704 | tf_op jit(solution)/shard_map/all_gather | solution.py:67
  10.0 121.7 %all-gather.8.cloned.1.call-start = ((), (), s32[]{:S(2)}) async-start(), calls=%async_computation.2 | async-start | bytes 4718592 | tf_op jit(solution)/shard_map/all_gather | solution.py:65
  10.7 283.3 %all-gather.12.cloned.1.call-start = ((), (), s32[]{:S(2)}) async-start(), calls=%async_computation.5 | async-start | bytes 2162688 | tf_op jit(solution)/shard_map/all_gather | solution.py:68
  11.5 296.9 %all-gather.10.cloned.1.call-start = ((), (), s32[]{:S(2)}) async-start(), calls=%async_computation.3 | async-start | bytes 2162688 | tf_op jit(solution)/shard_map/all_gather | solution.py:144
  12.4 0.5 copy-start.13
  16.2 129.8 %copy-start.9 = (f32[8]{0:T(128)S(1)}, f32[8]{0:T(128)}, u32[]{:S(2)}) copy-start(f32[8]{0:T(128)} %param.20) | copy-start | bytes 100
  139.5 12.9 %copy-start.1 = (bf16[1024,776]{1,0:T(8,128)(2,1)}, bf16[1024,776]{1,0:T(8,128)(2,1)S(1)}, u32[]{:S(2)}) copy-start(bf16[1024,776]{1,0:T(8,128)(2,1)S(1)} %convert_bitcast_fusion) | copy-start | bytes 4767748
  139.6 12.9 %collective-permute-start.1 = (bf16[3,256]{1,0:T(4,128)(2,1)S(1)}, bf16[3,256]{1,0:T(4,128)(2,1)S(1)}, u32[]{:S(2)}, u32[]{:S(2)}) collective-permute-start(bf16[3,256]{1,0:T(4,128)(2,1)S(1)} %slice.235), channel_id=1, source_target_pairs={{0,8},{8,16},{16,24},{24,32},{32,40},{40,48},{48,56},{56,64},{64,7... | collective-permute-start | bytes 4616 | tf_op jit(solution)/shard_map/ppermute | solution.py:13
  142.7 12.9 %collective-permute-start = (bf16[3,512]{1,0:T(4,128)(2,1)S(1)}, bf16[3,512]{1,0:T(4,128)(2,1)S(1)}, u32[]{:S(2)}, u32[]{:S(2)}) collective-permute-start(bf16[3,512]{1,0:T(4,128)(2,1)S(1)} %slice.226), channel_id=1, source_target_pairs={{0,8},{8,16},{16,24},{24,32},{32,40},{40,48},{48,56},{56,64},{64,7... | collective-permute-start | bytes 9224 | tf_op jit(solution)/shard_map/ppermute | solution.py:13
  154.0 1.6 slice-start
  161.3 3.0 copy-start.5
  164.0 20.0 %copy-start.10 = (f32[8]{0:T(128)S(1)}, f32[8]{0:T(128)}, u32[]{:S(2)}) copy-start(f32[8]{0:T(128)} %param.21) | copy-start | bytes 100
  164.2 45.1 %copy-start.6 = (f32[1,8]{1,0:T(1,128)S(1)}, f32[1,8]{1,0:T(1,128)}, u32[]{:S(2)}) copy-start(f32[1,8]{1,0:T(1,128)} %get-tuple-element.24) | copy-start | bytes 100
  164.2 45.1 %copy-start.7 = (f32[1,8]{1,0:T(1,128)S(1)}, f32[1,8]{1,0:T(1,128)}, u32[]{:S(2)}) copy-start(f32[1,8]{1,0:T(1,128)} %get-tuple-element.28) | copy-start | bytes 100
  164.2 45.1 %copy-start.8 = (f32[1,8]{1,0:T(1,128)S(1)}, f32[1,8]{1,0:T(1,128)}, u32[]{:S(2)}) copy-start(f32[1,8]{1,0:T(1,128)} %get-tuple-element.29) | copy-start | bytes 100
  164.4 14.2 %collective-permute-start.2 = (f32[8,129,64]{1,2,0:T(8,128)S(1)}, f32[8,129,64]{1,2,0:T(8,128)}, u32[]{:S(2)}, u32[]{:S(2)}) collective-permute-start(f32[8,129,64]{1,2,0:T(8,128)S(1)} %pad_maximum_fusion.1), channel_id=1, source_target_pairs={{0,8},{8,16},{16,24},{24,32},{32,40},{40,48},{48,56},{56,64},{64,7... | collective-permute-start | bytes 792584 | tf_op jit(solution)/shard_map/ppermute | solution.py:13
  178.5 20.3 %collective-permute-start.3 = (f32[8,129,64]{1,2,0:T(8,128)}, f32[8,129,64]{1,2,0:T(8,128)S(1)}, u32[]{:S(2)}, u32[]{:S(2)}) collective-permute-start(f32[8,129,64]{1,2,0:T(8,128)} %collective-permute-done.2), channel_id=1, source_target_pairs={{0,8},{8,16},{16,24},{24,32},{32,40},{40,48},{48,56},{56,64},{64,7... | collective-permute-start | bytes 792584 | tf_op jit(solution)/shard_map/ppermute | solution.py:13
  182.8 190.2 %reduce-scatter.2.cloned.1.call-start = ((), (), s32[]{:S(2)}) async-start(), calls=%async_computation.4 | async-start | bytes 9510912 | tf_op jit(solution)/shard_map/reduce_scatter | solution.py:150
  198.8 0.8 copy-start.3
  200.6 39.9 %copy-start.2 = (bf16[1024,128]{1,0:T(8,128)(2,1)S(1)}, bf16[1024,128]{1,0:T(8,128)(2,1)}, u32[]{:S(2)}) copy-start(bf16[1024,128]{1,0:T(8,128)(2,1)} %get-tuple-element.13) | copy-start | bytes 786436
  201.8 29.3 %collective-permute-start.4 = (f32[8,129,64]{1,2,0:T(8,128)S(1)}, f32[8,129,64]{1,2,0:T(8,128)S(1)}, u32[]{:S(2)}, u32[]{:S(2)}) collective-permute-start(f32[8,129,64]{1,2,0:T(8,128)S(1)} %pad_maximum_fusion.2), channel_id=1, source_target_pairs={{0,16},{8,24},{16,32},{24,40},{32,48},{40,56},{48,64},{56,72},{64,... | collective-permute-start | bytes 792584 | tf_op jit(solution)/shard_map/ppermute | solution.py:13
  231.4 33.1 %collective-permute-start.5 = (f32[8,129,64]{1,2,0:T(8,128)S(1)}, f32[8,129,64]{1,2,0:T(8,128)S(1)}, u32[]{:S(2)}, u32[]{:S(2)}) collective-permute-start(f32[8,129,64]{1,2,0:T(8,128)S(1)} %pad_maximum_fusion.3), channel_id=1, source_target_pairs={{0,32},{8,40},{16,48},{24,56},{32,64},{40,72},{48,80},{56,88},{64,... | collective-permute-start | bytes 792584 | tf_op jit(solution)/shard_map/ppermute | solution.py:13
  264.7 18.0 %collective-permute-start.6 = (f32[8,129,64]{1,2,0:T(8,128)S(1)}, f32[8,129,64]{1,2,0:T(8,128)S(1)}, u32[]{:S(2)}, u32[]{:S(2)}) collective-permute-start(f32[8,129,64]{1,2,0:T(8,128)S(1)} %pad_maximum_fusion.4), channel_id=1, source_target_pairs={{0,64},{8,72},{16,80},{24,88},{32,96},{40,104},{48,112},{56,120},{... | collective-permute-start | bytes 792584 | tf_op jit(solution)/shard_map/ppermute | solution.py:13
  282.8 1.2 copy-start
  294.0 14.4 %copy-start.4 = (f32[512]{0:T(512)S(1)}, f32[512]{0:T(512)}, u32[]{:S(2)}) copy-start(f32[512]{0:T(512)} %param.22) | copy-start | bytes 6148
  316.3 0.7 copy-start.11
  316.3 0.7 copy-start.12
  316.3 0.8 copy-start.14
Sparse Core Ops, SparseCore 0:
  10.1 80.4 all-gather.5
  92.5 39.1 all-gather.7
  134.3 75.4 all-gather.11
  212.2 96.1 all-gather.9
  316.4 56.5 reduce-scatter.1
where the time goes:
time: 384 us; the launch traced here: 383 us
  waiting for transfers between devices  257 us (67%)
  starting transfers between devices  38.9 us (10%)
  other arithmetic  25.9 us (7%)
  matrix products  24.1 us (6%)
  local copies, waits for them, and re-layouts  22.1 us (6%)
  between operations  14.2 us (4%)
    ppermute x7, waiting for transfers between devices, passed_along(): return lax.ppermute(value, axis, pairs)  77.4 us
    all_gather x1, waiting for transfers between devices, on_device(): first_weights = lax.all_gather(first_cols, 'seq', axis=0, tiled=True)  74.5 us
    reduce_scatter x1, waiting for transfers between devices, on_device(): lax.psum_scatter(jnp.concatenate([partial_out, square_rows], axis=0), 'tp...  55.8 us
    all_gather x1, waiting for transfers between devices, on_device(): whole = lax.all_gather(tokens, 'tp', axis=1, tiled=True)  41.1 us
    ppermute x7, starting transfers between devices, passed_along(): return lax.ppermute(value, axis, pairs)  38.7 us
    all_gather x1, waiting for transfers between devices, on_device(): lax.all_gather(w_output, 'seq', axis=1, tiled=True)  7.9 us
    dot_general x1, matrix products, on_device(): jnp.dot(whole, first_weights, preferred_element_type=jnp.float32)  7.8 us
  transfers between devices with their start and end apart: 12, of which 9 were waited for; matrix products, arithmetic and copies ran while one was open for 14% of the time, Pallas kernels for 0%

commit v1 on v0

--- a/solution.py
+++ b/solution.py
@@ -64,7 +64,9 @@
     carry_on = jnp.repeat(local_start == 0, BLOCK)
     whole = lax.all_gather(tokens, "tp", axis=1, tiled=True)
     first_cols = jnp.concatenate([w_inner[:, 1, :], w_states, w_step], axis=1)
-    first_weights = lax.all_gather(first_cols, "seq", axis=0, tiled=True)
+    first_weights = jnp.concatenate(
+        lax.all_to_all(jnp.stack([first_cols] * lax.axis_size("seq")), "seq", 0, 0), axis=0
+    )
     gate_weights = lax.all_gather(w_inner[:, 0, :], "seq", axis=0, tiled=True)
     first_sum = jnp.dot(whole, first_weights, preferred_element_type=jnp.float32)
     projected = first_sum.astype(jnp.bfloat16)

time: 384 us -> 349 us (0.909)
  waiting for transfers between devices: 257 us -> 193 us
  starting transfers between devices: 38.9 us -> 70 us
    all_to_all x0 -> x1, waiting for transfers between devices: none -> 81.5 us  [on_device(): lax.all_to_all(jnp.stack([first_cols] * lax.axis_size('seq')), 'seq', 0, 0)]
    all_gather x1 -> x0, waiting for transfers between devices: 74.5 us -> none  [on_device(): first_weights = lax.all_gather(first_cols, 'seq', axis=0, tiled=True)]
    all_gather x1, waiting for transfers between devices: 41.1 us -> 0.01 us  [on_device(): whole = lax.all_gather(tokens, 'tp', axis=1, tiled=True)]
    ppermute x7, waiting for transfers between devices: 77.4 us -> 52.3 us  [passed_along(): return lax.ppermute(value, axis, pairs)]
    ppermute x7, starting transfers between devices: 38.7 us -> 57.8 us  [passed_along(): return lax.ppermute(value, axis, pairs)]
    all_to_all x0 -> x1, starting transfers between devices: none -> 12.1 us  [on_device(): lax.all_to_all(jnp.stack([first_cols] * lax.axis_size('seq')), 'seq', 0, 0)]
    all_gather x1, waiting for transfers between devices: 7.9 us -> 0.02 us  [on_device(): lax.all_gather(w_output, 'seq', axis=1, tiled=True)]
  transfers between devices with their start and end apart: 12 -> 12, of which waited for: 9 -> 7; matrix products, arithmetic and copies ran while one was open for 14% -> 17% of each run, Pallas kernels for 0% -> 0%
where the time goes in v1:
time: 349 us; the launch traced here: 348 us
  waiting for transfers between devices  193 us (55%)
  starting transfers between devices  70 us (20%)
  other arithmetic  24.2 us (7%)
  matrix products  24 us (7%)
  local copies, waits for them, and re-layouts  22.9 us (7%)
  between operations  14.4 us (4%)
    all_to_all x1, waiting for transfers between devices, on_device(): lax.all_to_all(jnp.stack([first_cols] * lax.axis_size('seq')), 'seq', 0, 0)  81.5 us
    reduce_scatter x1, waiting for transfers between devices, on_device(): lax.psum_scatter(jnp.concatenate([partial_out, square_rows], axis=0), 'tp...  57.9 us
    ppermute x7, starting transfers between devices, passed_along(): return lax.ppermute(value, axis, pairs)  57.8 us
    ppermute x7, waiting for transfers between devices, passed_along(): return lax.ppermute(value, axis, pairs)  52.3 us
    all_to_all x1, starting transfers between devices, on_device(): lax.all_to_all(jnp.stack([first_cols] * lax.axis_size('seq')), 'seq', 0, 0)  12.1 us
    dot_general x1, matrix products, on_device(): jnp.dot(whole, first_weights, preferred_element_type=jnp.float32)  7.82 us
    reshape x2, local copies, waits for them, and re-layouts, on_device(): (y_inner + y_carry).reshape(row_count, inner_here)  7.59 us
  transfers between devices with their start and end apart: 12, of which 7 were waited for; matrix products, arithmetic and copies ran while one was open for 17% of the time, Pallas kernels for 0%

profile of v1, /device:TPU:1, one launch (start us, length us, event | category | flops | bytes accessed | tf_op | source)
XLA Modules:
  0.0 348.1 jit_solution(10061974807545702585)
XLA Ops:
  6.5 0.7 all-gather.5.cloned.1.call-update
  7.3 0.8 copy.88
  8.0 1.2 fusion.70
  9.3 0.8 pad_maximum_fusion.5
  10.0 2.4 stack.10
  12.5 12.1 %all-to-all-start = ((bf16[32,64,776]{2,1,0:T(8,128)(2,1)}), bf16[32,64,776]{2,1,0:T(8,128)(2,1)}, u32[]{:S(2)}, u32[]{:S(2)}) async-start(bf16[32,64,776]{2,1,0:T(8,128)(2,1)} %stack.10), calls=%async_computation | async-start | bytes 7340032 | tf_op jit(solution)/shard_map/all_to_all | solution.py:68
  24.6 0.6 copy.109
  26.4 0.7 fusion.73
  27.1 81.5 %all-to-all-done = bf16[32,64,776]{2,1,0:T(8,128)(2,1)} async-done(((bf16[32,64,776]{2,1,0:T(8,128)(2,1)}), bf16[32,64,776]{2,1,0:T(8,128)(2,1)}, u32[]{:S(2)}, u32[]{:S(2)}) %all-to-all-start) | async-done | bytes 3178528 | tf_op jit(solution)/shard_map/all_to_all | solution.py:68
  108.6 7.8 %convert_bitcast_fusion = bf16[1024,776]{1,0:T(8,128)(2,1)S(1)} fusion(bf16[2048,776]{1,0:T(8,128)(2,1)} %bitcast.1, bf16[1024,2048]{1,0:T(8,128)(2,1)} %all-gather.5.cloned.1.call-done), kind=kOutput, calls=%fused_computation.36 | convolution fusion | flops 3255574528 | bytes 8962048 | tf_op jit(solution)/shard_map/dot_general | solution.py:71
  116.5 3.9 %collective-permute-start.1 = (bf16[3,256]{1,0:T(4,128)(2,1)S(1)}, bf16[3,256]{1,0:T(4,128)(2,1)S(1)}, u32[]{:S(2)}, u32[]{:S(2)}) collective-permute-start(bf16[3,256]{1,0:T(4,128)(2,1)S(1)} %slice.235), channel_id=1, source_target_pairs={{0,8},{8,16},{16,24},{24,32},{32,40},{40,48},{48,56},{56,64},{64,7... | collective-permute-start | bytes 4616 | tf_op jit(solution)/shard_map/ppermute | solution.py:13
  120.4 4.0 %collective-permute-start = (bf16[3,512]{1,0:T(4,128)(2,1)S(1)}, bf16[3,512]{1,0:T(4,128)(2,1)S(1)}, u32[]{:S(2)}, u32[]{:S(2)}) collective-permute-start(bf16[3,512]{1,0:T(4,128)(2,1)S(1)} %slice.226), channel_id=1, source_target_pairs={{0,8},{8,16},{16,24},{24,32},{32,40},{40,48},{48,56},{56,64},{64,7... | collective-permute-start | bytes 9224 | tf_op jit(solution)/shard_map/ppermute | solution.py:13
  125.1 2.3 reduce-window.6
  128.4 2.4 broadcast_multiply_fusion.3
  131.1 1.4 multiply_convert_fusion.9
  132.6 0.7 fusion.69
  133.3 0.8 convert_element_type.64
  134.5 2.2 multiply_convert_fusion.5
  136.7 1.1 reshape.179
  137.8 1.9 copy.95
  139.8 2.8 fusion.11
  142.9 4.6 %collective-permute-start.2 = (f32[8,129,64]{1,2,0:T(8,128)S(1)}, f32[8,129,64]{1,2,0:T(8,128)}, u32[]{:S(2)}, u32[]{:S(2)}) collective-permute-start(f32[8,129,64]{1,2,0:T(8,128)S(1)} %pad_maximum_fusion.1), channel_id=1, source_target_pairs={{0,8},{8,16},{16,24},{24,32},{32,40},{40,48},{48,56},{56,64},{64,7... | collective-permute-start | bytes 792584 | tf_op jit(solution)/shard_map/ppermute | solution.py:13
  147.4 9.2 %collective-permute-done.2 = f32[8,129,64]{1,2,0:T(8,128)} collective-permute-done((f32[8,129,64]{1,2,0:T(8,128)S(1)}, f32[8,129,64]{1,2,0:T(8,128)}, u32[]{:S(2)}, u32[]{:S(2)}) %collective-permute-start.2) | collective-permute-done | bytes 264224 | tf_op jit(solution)/shard_map/ppermute | solution.py:13
  156.6 4.2 %collective-permute-start.3 = (f32[8,129,64]{1,2,0:T(8,128)}, f32[8,129,64]{1,2,0:T(8,128)S(1)}, u32[]{:S(2)}, u32[]{:S(2)}) collective-permute-start(f32[8,129,64]{1,2,0:T(8,128)} %collective-permute-done.2), channel_id=1, source_target_pairs={{0,8},{8,16},{16,24},{24,32},{32,40},{40,48},{48,56},{56,64},{64,7... | collective-permute-start | bytes 792584 | tf_op jit(solution)/shard_map/ppermute | solution.py:13
  161.6 0.7 pad.14.clone
  162.5 0.9 slice_reduce_fusion.4
  163.4 6.8 %collective-permute-done.3 = f32[8,129,64]{1,2,0:T(8,128)S(1)} collective-permute-done((f32[8,129,64]{1,2,0:T(8,128)}, f32[8,129,64]{1,2,0:T(8,128)S(1)}, u32[]{:S(2)}, u32[]{:S(2)}) %collective-permute-start.3) | collective-permute-done | bytes 264224 | tf_op jit(solution)/shard_map/ppermute | solution.py:13
  170.3 0.8 copy-done.3
  171.1 1.0 slice_add_fusion
  172.1 1.1 slice_multiply_fusion.7
  173.3 4.3 %collective-permute-start.4 = (f32[8,129,64]{1,2,0:T(8,128)S(1)}, f32[8,129,64]{1,2,0:T(8,128)S(1)}, u32[]{:S(2)}, u32[]{:S(2)}) collective-permute-start(f32[8,129,64]{1,2,0:T(8,128)S(1)} %pad_maximum_fusion.2), channel_id=1, source_target_pairs={{0,16},{8,24},{16,32},{24,40},{32,48},{40,56},{48,64},{56,72},{64,... | collective-permute-start | bytes 792584 | tf_op jit(solution)/shard_map/ppermute | solution.py:13
  177.8 15.7 %collective-permute-done.4 = f32[8,129,64]{1,2,0:T(8,128)S(1)} collective-permute-done((f32[8,129,64]{1,2,0:T(8,128)S(1)}, f32[8,129,64]{1,2,0:T(8,128)S(1)}, u32[]{:S(2)}, u32[]{:S(2)}) %collective-permute-start.4) | collective-permute-done | bytes 264224 | tf_op jit(solution)/shard_map/ppermute | solution.py:13
  193.8 8.2 %collective-permute-start.5 = (f32[8,129,64]{1,2,0:T(8,128)S(1)}, f32[8,129,64]{1,2,0:T(8,128)S(1)}, u32[]{:S(2)}, u32[]{:S(2)}) collective-permute-start(f32[8,129,64]{1,2,0:T(8,128)S(1)} %pad_maximum_fusion.3), channel_id=1, source_target_pairs={{0,32},{8,40},{16,48},{24,56},{32,64},{40,72},{48,80},{56,88},{64,... | collective-permute-start | bytes 792584 | tf_op jit(solution)/shard_map/ppermute | solution.py:13
  202.5 6.9 %collective-permute-done.5 = f32[8,129,64]{1,2,0:T(8,128)S(1)} collective-permute-done((f32[8,129,64]{1,2,0:T(8,128)S(1)}, f32[8,129,64]{1,2,0:T(8,128)S(1)}, u32[]{:S(2)}, u32[]{:S(2)}) %collective-permute-start.5) | collective-permute-done | bytes 264224 | tf_op jit(solution)/shard_map/ppermute | solution.py:13
  209.6 28.6 %collective-permute-start.6 = (f32[8,129,64]{1,2,0:T(8,128)S(1)}, f32[8,129,64]{1,2,0:T(8,128)S(1)}, u32[]{:S(2)}, u32[]{:S(2)}) collective-permute-start(f32[8,129,64]{1,2,0:T(8,128)S(1)} %pad_maximum_fusion.4), channel_id=1, source_target_pairs={{0,64},{8,72},{16,80},{24,88},{32,96},{40,104},{48,112},{56,120},{... | collective-permute-start | bytes 792584 | tf_op jit(solution)/shard_map/ppermute | solution.py:13
  238.2 2.0 broadcast_multiply_fusion.1
  240.4 13.7 %collective-permute-done.6 = f32[8,129,64]{1,2,0:T(8,128)S(1)} collective-permute-done((f32[8,129,64]{1,2,0:T(8,128)S(1)}, f32[8,129,64]{1,2,0:T(8,128)S(1)}, u32[]{:S(2)}, u32[]{:S(2)}) %collective-permute-start.6) | collective-permute-done | bytes 264224 | tf_op jit(solution)/shard_map/ppermute | solution.py:13
  254.8 0.6 copy-done
  255.4 2.4 bitcast_add_fusion
  257.8 2.8 copy.104
  260.6 4.8 %reshape.178 = f32[1024,512]{1,0:T(8,128)} reshape(f32[4,256,8,64]{3,2,1,0:T(8,128)} %copy.104) | data formatting | bytes 4194304 | tf_op jit(solution)/shard_map/reshape | solution.py:138
  265.4 6.3 %multiply_reduce_fusion = (f32[1024]{0:T(1024)S(1)}, f32[1024,512]{1,0:T(8,128)S(1)}) fusion(bf16[1024,2048]{1,0:T(8,128)(2,1)} %all-gather.5.cloned.1.call-done, bf16[2048,1,512]{2,0,1:T(8,128)(2,1)} %all-gather.9.cloned.1.call-done, f32[1024,512]{1,0:T(8,128)} %reshape.178, bf16[1024,512]{1,0:T(8,128)(2,1)S(1)} %multiply_convert_fusion.5, f32[512]{0:T(512)S(1)} %mul.490), kind=kOutput, calls=%fused_computation.31 | convolution fusion | flops 2153774080 | bytes 11540480 | tf_op jit(solution)/shard_map/dot_general | solution.py:76
  271.8 4.0 %fusion.28 = f32[1024,2048]{1,0:T(8,128)S(1)} fusion(bf16[512,2048]{0,1:T(8,128)(2,1)} %all-gather.7.cloned.1.call-done, f32[1024,512]{1,0:T(8,128)S(1)} %get-tuple-element.41, f32[512]{0:T(512)S(1)} %copy-done.4), kind=kOutput, calls=%fused_computation.40 | convolution fusion | flops 2148532224 | bytes 12584960 | tf_op jit(solution)/shard_map/dot_general | solution.py:144
  275.8 3.9 %pad_maximum_fusion = f32[1028,2048]{1,0:T(8,128)} fusion(f32[4,2048]{1,0:T(4,128)S(1)} %bitcast.120, f32[1024,2048]{1,0:T(8,128)S(1)} %fusion.28), kind=kLoop, calls=%fused_computation | loop fusion | flops 2105344 | bytes 16842752 | tf_op jit(solution)/shard_map/concatenate | solution.py:153
  279.7 0.6 copy-done.15
  280.6 57.9 %reduce-scatter.2.cloned.1.call-done = f32[1028,256]{1,0:T(8,128)} async-done(((f32[1028,2048]{1,0:T(8,128)}), f32[1028,256]{1,0:T(8,128)}) %reduce-scatter.2.cloned.1.call-update) | async-done | bytes 1052688 | tf_op jit(solution)/shard_map/reduce_scatter | solution.py:152
  338.5 0.7 fusion.50
  339.2 2.4 fusion.30
  (110 shorter events, 6.3 us)
Async XLA Ops:
  6.5 102.1 %all-gather.5.cloned.1.call-start = ((), (), s32[]{:S(2)}) async-start(), calls=%async_computation.2 | async-start | bytes 4718592 | tf_op jit(solution)/shard_map/all_gather | solution.py:65
  12.5 12.9 %copy-start.14 = (s32[128]{0:T(128)S(1)}, s32[128]{0:T(128)}, u32[]{:S(2)}) copy-start(s32[128]{0:T(128)} %param.24) | copy-start | bytes 1540
  12.5 13.8 %copy-start.13 = (f32[8]{0:T(128)S(1)}, f32[8]{0:T(128)}, u32[]{:S(2)}) copy-start(f32[8]{0:T(128)} %param.19) | copy-start | bytes 100
  12.5 14.6 %copy-start.6 = (f32[4,256]{1,0:T(4,128)S(1)}, f32[4,256]{1,0:T(4,128)}, u32[]{:S(2)}) copy-start(f32[4,256]{1,0:T(4,128)} %param.18) | copy-start | bytes 12292
  12.5 14.6 %copy-start.5 = (f32[4,512]{1,0:T(4,128)S(1)}, f32[4,512]{1,0:T(4,128)}, u32[]{:S(2)}) copy-start(f32[4,512]{1,0:T(4,128)} %param.17) | copy-start | bytes 24580
  12.5 96.2 %all-to-all-start = ((bf16[32,64,776]{2,1,0:T(8,128)(2,1)}), bf16[32,64,776]{2,1,0:T(8,128)(2,1)}, u32[]{:S(2)}, u32[]{:S(2)}) async-start(bf16[32,64,776]{2,1,0:T(8,128)(2,1)} %stack.10), calls=%async_computation | async-start | bytes 7340032 | tf_op jit(solution)/shard_map/all_to_all | solution.py:68
  24.6 240.8 %all-gather.9.cloned.1.call-start = ((), (), s32[]{:S(2)}) async-start(), calls=%async_computation.5 | async-start | bytes 2162688 | tf_op jit(solution)/shard_map/all_gather | solution.py:70
  25.3 246.5 %all-gather.7.cloned.1.call-start = ((), (), s32[]{:S(2)}) async-start(), calls=%async_computation.3 | async-start | bytes 2162688 | tf_op jit(solution)/shard_map/all_gather | solution.py:146
  25.6 0.6 copy-start.17
  108.6 15.8 %copy-start.11 = (f32[8]{0:T(128)S(1)}, f32[8]{0:T(128)}, u32[]{:S(2)}) copy-start(f32[8]{0:T(128)} %param.20) | copy-start | bytes 100
  116.5 14.5 %copy-start.1 = (bf16[1024,776]{1,0:T(8,128)(2,1)}, bf16[1024,776]{1,0:T(8,128)(2,1)S(1)}, u32[]{:S(2)}) copy-start(bf16[1024,776]{1,0:T(8,128)(2,1)S(1)} %convert_bitcast_fusion) | copy-start | bytes 4767748
  116.5 14.5 %collective-permute-start.1 = (bf16[3,256]{1,0:T(4,128)(2,1)S(1)}, bf16[3,256]{1,0:T(4,128)(2,1)S(1)}, u32[]{:S(2)}, u32[]{:S(2)}) collective-permute-start(bf16[3,256]{1,0:T(4,128)(2,1)S(1)} %slice.235), channel_id=1, source_target_pairs={{0,8},{8,16},{16,24},{24,32},{32,40},{40,48},{48,56},{56,64},{64,7... | collective-permute-start | bytes 4616 | tf_op jit(solution)/shard_map/ppermute | solution.py:13
  120.4 13.8 %collective-permute-start = (bf16[3,512]{1,0:T(4,128)(2,1)S(1)}, bf16[3,512]{1,0:T(4,128)(2,1)S(1)}, u32[]{:S(2)}, u32[]{:S(2)}) collective-permute-start(bf16[3,512]{1,0:T(4,128)(2,1)S(1)} %slice.226), channel_id=1, source_target_pairs={{0,8},{8,16},{16,24},{24,32},{32,40},{40,48},{48,56},{56,64},{64,7... | collective-permute-start | bytes 9224 | tf_op jit(solution)/shard_map/ppermute | solution.py:13
  132.6 1.6 slice-start
  139.8 3.0 copy-start.7
  142.5 19.8 %copy-start.12 = (f32[8]{0:T(128)S(1)}, f32[8]{0:T(128)}, u32[]{:S(2)}) copy-start(f32[8]{0:T(128)} %param.21) | copy-start | bytes 100
  142.7 34.9 %copy-start.8 = (f32[1,8]{1,0:T(1,128)S(1)}, f32[1,8]{1,0:T(1,128)}, u32[]{:S(2)}) copy-start(f32[1,8]{1,0:T(1,128)} %get-tuple-element.24) | copy-start | bytes 100
  142.7 34.9 %copy-start.9 = (f32[1,8]{1,0:T(1,128)S(1)}, f32[1,8]{1,0:T(1,128)}, u32[]{:S(2)}) copy-start(f32[1,8]{1,0:T(1,128)} %get-tuple-element.28) | copy-start | bytes 100
  142.7 34.9 %copy-start.10 = (f32[1,8]{1,0:T(1,128)S(1)}, f32[1,8]{1,0:T(1,128)}, u32[]{:S(2)}) copy-start(f32[1,8]{1,0:T(1,128)} %get-tuple-element.29) | copy-start | bytes 100
  142.9 13.8 %collective-permute-start.2 = (f32[8,129,64]{1,2,0:T(8,128)S(1)}, f32[8,129,64]{1,2,0:T(8,128)}, u32[]{:S(2)}, u32[]{:S(2)}) collective-permute-start(f32[8,129,64]{1,2,0:T(8,128)S(1)} %pad_maximum_fusion.1), channel_id=1, source_target_pairs={{0,8},{8,16},{16,24},{24,32},{32,40},{40,48},{48,56},{56,64},{64,7... | collective-permute-start | bytes 792584 | tf_op jit(solution)/shard_map/ppermute | solution.py:13
  156.6 13.6 %collective-permute-start.3 = (f32[8,129,64]{1,2,0:T(8,128)}, f32[8,129,64]{1,2,0:T(8,128)S(1)}, u32[]{:S(2)}, u32[]{:S(2)}) collective-permute-start(f32[8,129,64]{1,2,0:T(8,128)} %collective-permute-done.2), channel_id=1, source_target_pairs={{0,8},{8,16},{16,24},{24,32},{32,40},{40,48},{48,56},{56,64},{64,7... | collective-permute-start | bytes 792584 | tf_op jit(solution)/shard_map/ppermute | solution.py:13
  160.9 177.6 %reduce-scatter.2.cloned.1.call-start = ((), (), s32[]{:S(2)}) async-start(), calls=%async_computation.4 | async-start | bytes 9510912 | tf_op jit(solution)/shard_map/reduce_scatter | solution.py:152
  170.3 0.8 copy-start.3
  172.1 29.9 %copy-start.2 = (bf16[1024,128]{1,0:T(8,128)(2,1)S(1)}, bf16[1024,128]{1,0:T(8,128)(2,1)}, u32[]{:S(2)}) copy-start(bf16[1024,128]{1,0:T(8,128)(2,1)} %get-tuple-element.13) | copy-start | bytes 786436
  173.3 20.3 %collective-permute-start.4 = (f32[8,129,64]{1,2,0:T(8,128)S(1)}, f32[8,129,64]{1,2,0:T(8,128)S(1)}, u32[]{:S(2)}, u32[]{:S(2)}) collective-permute-start(f32[8,129,64]{1,2,0:T(8,128)S(1)} %pad_maximum_fusion.2), channel_id=1, source_target_pairs={{0,16},{8,24},{16,32},{24,40},{32,48},{40,56},{48,64},{56,72},{64,... | collective-permute-start | bytes 792584 | tf_op jit(solution)/shard_map/ppermute | solution.py:13
  193.8 15.6 %collective-permute-start.5 = (f32[8,129,64]{1,2,0:T(8,128)S(1)}, f32[8,129,64]{1,2,0:T(8,128)S(1)}, u32[]{:S(2)}, u32[]{:S(2)}) collective-permute-start(f32[8,129,64]{1,2,0:T(8,128)S(1)} %pad_maximum_fusion.3), channel_id=1, source_target_pairs={{0,32},{8,40},{16,48},{24,56},{32,64},{40,72},{48,80},{56,88},{64,... | collective-permute-start | bytes 792584 | tf_op jit(solution)/shard_map/ppermute | solution.py:13
  209.6 44.4 %collective-permute-start.6 = (f32[8,129,64]{1,2,0:T(8,128)S(1)}, f32[8,129,64]{1,2,0:T(8,128)S(1)}, u32[]{:S(2)}, u32[]{:S(2)}) collective-permute-start(f32[8,129,64]{1,2,0:T(8,128)S(1)} %pad_maximum_fusion.4), channel_id=1, source_target_pairs={{0,64},{8,72},{16,80},{24,88},{32,96},{40,104},{48,112},{56,120},{... | collective-permute-start | bytes 792584 | tf_op jit(solution)/shard_map/ppermute | solution.py:13
  254.2 1.2 copy-start
  265.4 6.4 %copy-start.4 = (f32[512]{0:T(512)S(1)}, f32[512]{0:T(512)}, u32[]{:S(2)}) copy-start(f32[512]{0:T(512)} %param.22) | copy-start | bytes 6148
  279.7 0.7 copy-start.15
  279.7 0.7 copy-start.16
  279.7 0.8 copy-start.18
Sparse Core Ops, SparseCore 0:
  9.2 42.2 all-gather.4
  54.1 82.0 all-gather.8
  161.0 100.1 all-gather.6
  279.8 58.6 reduce-scatter.1
